TPU v7x, 128 devices: a whole 4x4x4 slice. The times are simulated.
128 devices in a mesh: obs: 8 (over z, core), tile: 16 (over x, y).
Axes of the slice: x: 4, y: 4, z: 4, core: 2. Of those that a mesh axis runs over, the one named last changes fastest.
Arguments:
- raw_obs: bfloat16 [4096, 128, 128], P(('obs', 'tile')), may hold values from -6 to 6
- obs_bias: bfloat16 [4096, 128], P(('obs', 'tile')), may hold values from -2 to 302
- instrument: int32 [4096], P(('obs', 'tile')), may hold values from 0 to 5
- owner: int32 [4096, 1], P(('obs', 'tile')), may hold values from 0 to 15; in each aligned block of 32 rows (0 to 31, 32 to 63, ...) at most 4 rows name the same one
- local_tile: int32 [4096], P(('obs', 'tile')), may hold values from 0 to 3
- latents: bfloat16 [8192, 512], P('tile'), may hold values from -6 to 6
- first_weight: bfloat16 [6, 128, 512], replicated, may hold values from -0.5 to 0.5
- second_weight: bfloat16 [6, 512, 512], replicated, may hold values from -0.25 to 0.25
- query_weight: bfloat16 [512, 512], replicated, may hold values from -0.25 to 0.25
- pair_weight: bfloat16 [512, 1024], replicated, may hold values from -0.25 to 0.25
- self_bias: float32 [8], replicated, may hold values from 6 to 9
- out_weight: bfloat16 [512, 512], P(None, 'obs'), may hold values from -0.25 to 0.25
- edge_gain: float32 [512], P('obs'), may hold values from 0.1 to 0.4
Outputs:
- joined_latents: float32 [8192, 512], P('tile', 'obs')
Inputs may be any that keep to these rules, and one draw needn't show every extreme that they name: Among the 32 blocks of one device, at most 4 have the same owner, and in every draw some device has exactly 4 blocks for one owner.
All inputs are finite; a program needn't handle non-finite values.
Results may differ from a plain program's by a relative error of at most 0.0036.
Values may be sent and summed in bfloat16 or wider, within the bound.
No kernel may reach another device: no remote copies, remote signals or barrier semaphores. Data moves between devices by JAX's collectives and lax.ppermute only.
A program may use at most 128 MiB of HBM per device.

v0:
```python
import functools

import jax
import jax.numpy as jnp
from jax import lax
from jax.experimental import pallas as pl
from jax.experimental.pallas import tpu as pltpu
from jax.sharding import PartitionSpec as P

TILE_DEV = 4
NEG_FLOOR = -1e30
INTERPRET = False


def extended(cells, sides, width):
    for axis, dim in sides:
        count = lax.axis_size(axis)
        head = lax.slice_in_dim(cells, 0, width, axis=dim)
        tail = lax.slice_in_dim(cells, cells.shape[dim] - width, cells.shape[dim], axis=dim)
        cells = jnp.concatenate(
            [
                lax.ppermute(tail, axis, [(i, (i + 1) % count) for i in range(count)]),
                cells,
                lax.ppermute(head, axis, [((i + 1) % count, i) for i in range(count)]),
            ],
            axis=dim,
        )
    return cells


def attend_kernel(kind_ref, tile_ref, raw_ref, bias_ref, w1_ref, w2_ref, kwt_ref, vw_ref, q_ref,
                  m_ref, l_ref, acc_ref, enc_ref, qs_ref, kbd_ref, vbd_ref, p_ref, *, heads, depth):
    slot = pl.program_id(0)

    @pl.when(slot == 0)
    def _():
        m_ref[...] = jnp.full(m_ref.shape, NEG_FLOOR, jnp.float32)
        l_ref[...] = jnp.zeros(l_ref.shape, jnp.float32)
        acc_ref[...] = jnp.zeros(acc_ref.shape, jnp.float32)

    tile = tile_ref[slot]
    kind = kind_ref[slot]
    width = heads * depth
    block_rows = enc_ref.shape[0]
    for k in range(w1_ref.shape[0]):
        @pl.when((tile >= 0) & (kind == k))
        def _():
            pre = jnp.dot(raw_ref[0], w1_ref[k], preferred_element_type=jnp.float32)
            hidden = (pre / (1.0 + jnp.exp(-pre))).astype(jnp.bfloat16)
            enc_ref[...] = jnp.dot(hidden, w2_ref[k], preferred_element_type=jnp.float32).astype(jnp.bfloat16)

    for j in range(q_ref.shape[0]):
        @pl.when(tile == j)
        def _():
            qs_ref[...] = q_ref[j]

    @pl.when(tile >= 0)
    def _():
        encoded = enc_ref[...]
        keys_t = lax.dot_general(
            kwt_ref[...], encoded, (((1,), (1,)), ((), ())), preferred_element_type=jnp.float32
        ).astype(jnp.bfloat16)
        values = jnp.dot(encoded, vw_ref[...], preferred_element_type=jnp.float32).astype(jnp.bfloat16)
        feature_row = lax.broadcasted_iota(jnp.int32, keys_t.shape, 0)
        feature_col = lax.broadcasted_iota(jnp.int32, values.shape, 1)
        for h in range(heads):
            rows = slice(h * block_rows, (h + 1) * block_rows)
            kbd_ref[:, rows] = jnp.where(
                (feature_row >= h * depth) & (feature_row < (h + 1) * depth), keys_t, jnp.zeros_like(keys_t)
            )
            vbd_ref[rows, :] = jnp.where(
                (feature_col >= h * depth) & (feature_col < (h + 1) * depth), values, jnp.zeros_like(values)
            )
        scores = jnp.dot(qs_ref[...], kbd_ref[...], preferred_element_type=jnp.float32)
        bias = bias_ref[0, 0:1, :].astype(jnp.float32)
        scale = depth ** (-0.5)
        peaks, sums = [], []
        for h in range(heads):
            rows = slice(h * block_rows, (h + 1) * block_rows)
            head_scores = scores[:, rows] * scale + bias
            peak = jnp.max(head_scores, axis=1, keepdims=True)
            weights = jnp.exp(head_scores - peak)
            peaks.append(peak)
            sums.append(jnp.sum(weights, axis=1, keepdims=True))
            p_ref[:, rows] = weights.astype(jnp.bfloat16)
        mixture = jnp.dot(p_ref[...], vbd_ref[...], preferred_element_type=jnp.float32)
        for j in range(q_ref.shape[0]):
            @pl.when(tile == j)
            def _():
                for h in range(heads):
                    cols = slice(h * depth, (h + 1) * depth)
                    old_peak = m_ref[j, :, h:h + 1]
                    new_peak = jnp.maximum(old_peak, peaks[h])
                    old_factor = jnp.exp(old_peak - new_peak)
                    new_factor = jnp.exp(peaks[h] - new_peak)
                    m_ref[j, :, h:h + 1] = new_peak
                    l_ref[j, :, h:h + 1] = l_ref[j, :, h:h + 1] * old_factor + sums[h] * new_factor
                    acc_ref[j, :, cols] = acc_ref[j, :, cols] * old_factor + mixture[:, cols] * new_factor


def attend_slots(kinds, tiles, packed, block_rows, first_weight, second_weight, pair_weight, queries, heads):
    slots, _, chans = packed.shape
    tiles_here, latent_rows, width = queries.shape
    depth = width // heads
    key_weight_t = pair_weight[:, :width].T
    value_weight = pair_weight[:, width:]
    const3 = lambda s: (0, 0, 0)
    const2 = lambda s: (0, 0)
    smem = pl.BlockSpec(memory_space=pltpu.SMEM)
    flops = slots * 2 * block_rows * (chans * first_weight.shape[2] + first_weight.shape[2] * width
                                      + width * 2 * width + 2 * latent_rows * width * heads)
    return pl.pallas_call(
        functools.partial(attend_kernel, heads=heads, depth=depth),
        grid=(slots,),
        in_specs=[
            smem,
            smem,
            pl.BlockSpec((1, block_rows, chans), lambda s: (s, 0, 0)),
            pl.BlockSpec((1, 8, chans), lambda s: (s, block_rows // 8, 0)),
            pl.BlockSpec(first_weight.shape, const3),
            pl.BlockSpec(second_weight.shape, const3),
            pl.BlockSpec(key_weight_t.shape, const2),
            pl.BlockSpec(value_weight.shape, const2),
            pl.BlockSpec(queries.shape, const3),
        ],
        out_specs=[
            pl.BlockSpec((tiles_here, latent_rows, heads), const3),
            pl.BlockSpec((tiles_here, latent_rows, heads), const3),
            pl.BlockSpec((tiles_here, latent_rows, width), const3),
        ],
        out_shape=[
            jax.ShapeDtypeStruct((tiles_here, latent_rows, heads), jnp.float32),
            jax.ShapeDtypeStruct((tiles_here, latent_rows, heads), jnp.float32),
            jax.ShapeDtypeStruct((tiles_here, latent_rows, width), jnp.float32),
        ],
        scratch_shapes=[
            pltpu.VMEM((block_rows, width), jnp.bfloat16),
            pltpu.VMEM((latent_rows, width), jnp.bfloat16),
            pltpu.VMEM((width, heads * block_rows), jnp.bfloat16),
            pltpu.VMEM((heads * block_rows, width), jnp.bfloat16),
            pltpu.VMEM((latent_rows, heads * block_rows), jnp.bfloat16),
        ],
        compiler_params=pltpu.CompilerParams(dimension_semantics=("arbitrary",)),
        cost_estimate=pl.CostEstimate(
            flops=int(flops), transcendentals=int(slots * block_rows * (first_weight.shape[2] + heads * latent_rows)),
            bytes_accessed=int(packed.size * 2 + first_weight.size * 2 + second_weight.size * 2
                               + pair_weight.size * 2 + queries.size * 2 + tiles_here * latent_rows * (width + 2 * heads) * 4),
        ),
        interpret=INTERPRET,
    )(kinds, tiles, packed, packed, first_weight, second_weight, key_weight_t, value_weight, queries)


def local(
    raw_obs,
    obs_bias,
    instrument,
    owner,
    local_tile,
    latents,
    first_weight,
    second_weight,
    query_weight,
    pair_weight,
    self_bias,
    out_weight,
    edge_gain,
):
    blocks, block_rows, chans = raw_obs.shape
    owners = lax.axis_size("tile")
    obs_count = lax.axis_size("obs")
    model_width = latents.shape[1]
    head_count = self_bias.shape[0]
    head_depth = model_width // head_count
    tiles_here = TILE_DEV
    slots_each = max(2, 2 * blocks // owners)
    slot_total = owners * slots_each

    targets = owner[:, 0]
    member = (targets[:, None] == jnp.arange(owners, dtype=jnp.int32)[None, :]).astype(jnp.int32)
    slot_rank = jnp.sum(jnp.cumsum(member, axis=0) * member, axis=1) - 1
    position = targets * slots_each + slot_rank
    select = (position[None, :] == jnp.arange(slot_total, dtype=jnp.int32)[:, None]).astype(jnp.bfloat16)
    lane = jnp.arange(chans, dtype=jnp.int32)[None, :]
    tag_row = jnp.where(lane == 0, (local_tile + 1)[:, None], jnp.where(lane == 1, instrument[:, None], 0))
    packed = jnp.concatenate(
        [
            raw_obs,
            obs_bias[:, None, :],
            tag_row[:, None, :].astype(jnp.bfloat16),
            jnp.zeros((blocks, 6, chans), jnp.bfloat16),
        ],
        axis=1,
    )
    placed = jnp.dot(select, packed.reshape(blocks, -1), preferred_element_type=jnp.float32)
    placed = placed.astype(jnp.bfloat16).reshape((slot_total,) + packed.shape[1:])
    received = lax.all_to_all(placed, "tile", split_axis=0, concat_axis=0, tiled=True)
    slot_tags = received[:, block_rows + 1, 0:2].astype(jnp.float32).astype(jnp.int32)
    slot_tiles = slot_tags[:, 0] - 1
    slot_kinds = slot_tags[:, 1]

    queries = jnp.dot(latents, query_weight, preferred_element_type=jnp.float32).astype(jnp.bfloat16)
    part_peak, part_sum, part_mix = attend_slots(
        slot_kinds, slot_tiles, received, block_rows, first_weight, second_weight, pair_weight,
        queries.reshape(tiles_here, -1, model_width), head_count,
    )

    row_total = latents.shape[0]
    share = row_total // obs_count
    partials = jnp.concatenate(
        [
            part_mix.reshape(row_total, model_width),
            part_peak.reshape(row_total, head_count),
            part_sum.reshape(row_total, head_count),
        ],
        axis=1,
    )
    mine = lax.all_to_all(partials, "obs", split_axis=0, concat_axis=0, tiled=True)
    mine = mine.reshape(obs_count, share, model_width + 2 * head_count)
    mix_o = mine[..., :model_width].reshape(obs_count, share, head_count, head_depth)
    peak_o = mine[..., model_width:model_width + head_count]
    sum_o = mine[..., model_width + head_count:]

    row_start = lax.axis_index("obs") * share
    latent_mine = lax.dynamic_slice_in_dim(latents, row_start, share, 0)
    query_mine = lax.dynamic_slice_in_dim(queries, row_start, share, 0).reshape(share, head_count, head_depth)
    self_pair = jnp.dot(latent_mine, pair_weight, preferred_element_type=jnp.float32).astype(jnp.bfloat16)
    self_keys = self_pair[:, :model_width].reshape(share, head_count, head_depth)
    self_values = self_pair[:, model_width:].reshape(share, head_count, head_depth)
    self_score = (
        jnp.sum(query_mine.astype(jnp.float32) * self_keys.astype(jnp.float32), axis=-1)
        * head_depth ** (-0.5)
        + self_bias
    )
    peak = jnp.maximum(jnp.max(peak_o, axis=0), self_score)
    factor_o = jnp.exp(peak_o - peak[None])
    factor_s = jnp.exp(self_score - peak)
    total = factor_s + jnp.sum(factor_o * sum_o, axis=0)
    mixture = factor_s[..., None] * self_values.astype(jnp.float32) + jnp.sum(
        factor_o[..., None] * mix_o, axis=0
    )
    attended = (mixture / total[..., None]).reshape(share, model_width).astype(jnp.bfloat16)
    attended = lax.all_gather(attended, "obs", axis=0, tiled=True)

    column_count = out_weight.shape[1]
    column_start = lax.axis_index("obs") * column_count
    latent_columns = lax.dynamic_slice_in_dim(latents, column_start, column_count, 1).astype(
        jnp.float32
    )
    updated = latent_columns + jnp.dot(attended, out_weight, preferred_element_type=jnp.float32)
    padded = extended(updated, (("tile", 0),), 1)
    return updated + edge_gain[None, :] * (padded[:-2] + padded[2:] - 2.0 * updated)


def solution(mesh):
    return jax.shard_map(
        local,
        mesh=mesh,
        in_specs=(
            P(("obs", "tile"), None, None),
            P(("obs", "tile"), None),
            P(("obs", "tile")),
            P(("obs", "tile"), None),
            P(("obs", "tile")),
            P("tile", None),
            P(),
            P(),
            P(),
            P(),
            P(),
            P(None, "obs"),
            P("obs"),
        ),
        out_specs=P("tile", "obs"),
        check_vma=False,
    )
```

profile of v0, /device:TPU:6, one launch (start us, length us, event | category | flops | bytes accessed | tf_op | source)
XLA Modules:
  0.0 228.9 jit_solution(13897415127695712483)
XLA Ops:
  0.0 0.7 broadcast_add_fusion
  0.7 0.7 copy.19
  1.4 0.7 fusion.14
  2.2 0.1 reduce_window_sum.11
  2.2 0.8 select_reduce_fusion
  3.1 0.7 add_add_fusion
  3.7 0.1 pad.10.clone
  3.8 0.8 fusion.12
  4.6 1.5 maximum_maximum_fusion
  6.1 0.7 fusion
  6.9 1.7 copy.25
  8.6 7.6 %all-to-all-start = ((bf16[64,136,128]{2,1,0:T(8,128)(2,1)}), bf16[64,136,128]{2,1,0:T(8,128)(2,1)}, u32[]{:S(2)}, u32[]{:S(2)}) async-start(bf16[64,136,128]{2,1,0:T(8,128)(2,1)} %bitcast.13), calls=%async_computation | async-start | bytes 4456448 | tf_op jit(solution)/shard_map/all_to_all | solution.py:196
  16.2 0.0 copy-start.4
  16.2 0.9 fusion.17
  17.0 1.0 copy.23
  18.1 1.2 convolution_convert_fusion.1
  19.3 26.2 %all-to-all-done.raw_ref.bias_ref = bf16[64,136,128]{2,1,0:T(8,128)(2,1)} async-done(((bf16[64,136,128]{2,1,0:T(8,128)(2,1)}), bf16[64,136,128]{2,1,0:T(8,128)(2,1)}, u32[]{:S(2)}, u32[]{:S(2)}) %all-to-all-start) | async-done | bytes 2228256 | tf_op jit(solution)/shard_map/all_to_all | solution.py:196
  45.5 0.9 fusion.10
  46.4 0.1 copy.20
  46.5 0.6 add_bitcast_fusion
  47.1 60.5 %shard_map.127 = (f32[4,128,8]{2,1,0:T(8,128)}, f32[4,128,8]{2,1,0:T(8,128)}, f32[4,128,512]{2,1,0:T(8,128)}) custom-call(s32[64]{0:T(128)} %get-tuple-element.20.kind_ref, s32[64]{0:T(128)} %get-tuple-element.19.tile_ref, bf16[64,136,128]{2,1,0:T(8,128)(2,1)} %all-to-all-done.raw_ref.bias_ref, bf16[64,136,128]{2,1,0:T(8,128)(2,1)} %all-to-all-done.raw_ref.bias_ref, ...), custom_call_target="tpu_custom_call" | custom-call | flops 31138512896 | bytes 8814592 | tf_op jit(solution)/shard_map/pallas_call | solution.py:112
  107.6 2.6 %pad_maximum_fusion = f32[8,64,528]{2,1,0:T(8,128)} fusion(f32[8,64,8]{2,1,0:T(8,128)} %bitcast.32, f32[8,64,8]{2,1,0:T(8,128)} %bitcast.31, f32[8,64,512]{2,1,0:T(8,128)} %bitcast.28), kind=kLoop, calls=%fused_computation.2 | loop fusion | flops 540672 | bytes 2162688 | tf_op jit(solution)/shard_map/concatenate | solution.py:209
  110.2 6.3 %all-to-all-start.1 = ((f32[8,64,528]{2,1,0:T(8,128)}), f32[8,64,528]{2,1,0:T(8,128)S(1)}, u32[]{:S(2)}, u32[]{:S(2)}) async-start(f32[8,64,528]{2,1,0:T(8,128)} %pad_maximum_fusion), calls=%async_computation.1 | async-start | bytes 2621440 | tf_op jit(solution)/shard_map/all_to_all | solution.py:217
  116.5 0.3 convolution_convert_fusion.2
  116.8 0.9 convert_multiply_fusion
  117.7 0.1 mul.81
  117.8 0.1 constant_dynamic-slice_fusion
  117.9 0.1 copy.22
  118.0 0.1 reduce_sum.36
  118.2 17.1 %all-to-all-done.1 = f32[8,64,528]{2,1,0:T(8,128)S(1)} async-done(((f32[8,64,528]{2,1,0:T(8,128)}), f32[8,64,528]{2,1,0:T(8,128)S(1)}, u32[]{:S(2)}, u32[]{:S(2)}) %all-to-all-start.1) | async-done | bytes 1081376 | tf_op jit(solution)/shard_map/all_to_all | solution.py:217
  135.3 0.1 fusion.4
  135.5 0.9 copy-done.1
  136.3 0.6 mul.90
  136.9 1.5 mul.91
  138.4 0.1 div.11
  138.5 0.1 div.12
  138.7 0.1 mul.87
  138.8 0.1 mul.88
  138.9 0.8 copy-done.2
  139.7 1.4 fusion.3
  141.1 0.0 copy-start.7
  141.2 13.1 %all_gather.3 = bf16[512,512]{1,0:T(8,128)(2,1)S(1)} all-gather(bf16[64,512]{1,0:T(8,128)(2,1)S(1)} %divide_convert_fusion), channel_id=1, replica_groups=mesh['obs'=8,'tile'=16] {'obs'}, dimensions={0}, use_global_device_ids=true | all-gather | bytes 589824 | tf_op jit(solution)/shard_map/all_gather | solution.py:242
  154.3 0.3 convolution_add_fusion
  154.6 0.1 fusion.18
  154.6 69.5 %collective-permute-start = (f32[1,64]{0,1:T(8,128)S(1)}, f32[1,64]{0,1:T(8,128)S(1)}, u32[]{:S(2)}, u32[]{:S(2)}) collective-permute-start(f32[1,64]{0,1:T(8,128)S(1)} %get-tuple-element.17), channel_id=1, source_target_pairs={{0,1},{1,2},{2,3},{3,4},{4,5},{5,6},{6,7},{7,8},{8,9},{9,10},{10,1... | collective-permute-start | bytes 776 | tf_op jit(solution)/shard_map/ppermute | solution.py:22
  224.2 1.6 collective-permute-done
  225.8 2.3 %collective-permute-done.1 = f32[1,64]{0,1:T(8,128)S(1)} collective-permute-done((f32[1,64]{0,1:T(8,128)S(1)}, f32[1,64]{0,1:T(8,128)S(1)}, u32[]{:S(2)}, u32[]{:S(2)}) %collective-permute-start.1) | collective-permute-done | bytes 288 | tf_op jit(solution)/shard_map/ppermute | solution.py:24
  228.1 0.8 fusion.8
  (19 shorter events, 0.1 us)
Async XLA Ops:
  0.0 18.1 %copy-start = (bf16[512,512]{1,0:T(8,128)(2,1)S(1)}, bf16[512,512]{1,0:T(8,128)(2,1)}, u32[]{:S(2)}) copy-start(bf16[512,512]{1,0:T(8,128)(2,1)} %param.18) | copy-start | bytes 1572868
  8.6 7.6 %copy-start.3 = (bf16[512,1024]{1,0:T(8,128)(2,1)S(1)}, bf16[512,1024]{1,0:T(8,128)(2,1)}, u32[]{:S(2)}) copy-start(bf16[512,1024]{1,0:T(8,128)(2,1)} %param.22) | copy-start | bytes 3145732
  8.6 36.9 %all-to-all-start = ((bf16[64,136,128]{2,1,0:T(8,128)(2,1)}), bf16[64,136,128]{2,1,0:T(8,128)(2,1)}, u32[]{:S(2)}, u32[]{:S(2)}) async-start(bf16[64,136,128]{2,1,0:T(8,128)(2,1)} %bitcast.13), calls=%async_computation | async-start | bytes 4456448 | tf_op jit(solution)/shard_map/all_to_all | solution.py:196
  16.2 1.9 copy-start.4
  110.2 25.1 %all-to-all-start.1 = ((f32[8,64,528]{2,1,0:T(8,128)}), f32[8,64,528]{2,1,0:T(8,128)S(1)}, u32[]{:S(2)}, u32[]{:S(2)}) async-start(f32[8,64,528]{2,1,0:T(8,128)} %pad_maximum_fusion), calls=%async_computation.1 | async-start | bytes 2621440 | tf_op jit(solution)/shard_map/all_to_all | solution.py:217
  116.5 18.8 %copy-start.6 = (f32[8]{0:T(128)S(1)}, f32[8]{0:T(128)}, u32[]{:S(2)}) copy-start(f32[8]{0:T(128)} %param.23) | copy-start | bytes 100
  135.3 1.1 copy-start.1
  138.4 1.3 copy-start.2
  139.7 14.6 %copy-start.5 = (bf16[512,64]{0,1:T(8,128)(2,1)S(1)}, bf16[512,64]{0,1:T(8,128)(2,1)}, u32[]{:S(2)}) copy-start(bf16[512,64]{0,1:T(8,128)(2,1)} %param.24) | copy-start | bytes 196612
  141.1 87.0 %copy-start.7 = (f32[64]{0:T(128)S(1)}, f32[64]{0:T(128)}, u32[]{:S(2)}) copy-start(f32[64]{0:T(128)} %param.25) | copy-start | bytes 772
  154.6 71.1 %collective-permute-start = (f32[1,64]{0,1:T(8,128)S(1)}, f32[1,64]{0,1:T(8,128)S(1)}, u32[]{:S(2)}, u32[]{:S(2)}) collective-permute-start(f32[1,64]{0,1:T(8,128)S(1)} %get-tuple-element.17), channel_id=1, source_target_pairs={{0,1},{1,2},{2,3},{3,4},{4,5},{5,6},{6,7},{7,8},{8,9},{9,10},{10,1... | collective-permute-start | bytes 776 | tf_op jit(solution)/shard_map/ppermute | solution.py:22
  224.2 3.9 %collective-permute-start.1 = (f32[1,64]{0,1:T(8,128)S(1)}, f32[1,64]{0,1:T(8,128)S(1)}, u32[]{:S(2)}, u32[]{:S(2)}) collective-permute-start(f32[1,64]{0,1:T(8,128)S(1)} %get-tuple-element.18), channel_id=1, source_target_pairs={{1,0},{2,1},{3,2},{4,3},{5,4},{6,5},{7,6},{8,7},{9,8},{10,9},{11,1... | collective-permute-start | bytes 776 | tf_op jit(solution)/shard_map/ppermute | solution.py:24
where the time goes:
time: 231 us; the launch traced here: 229 us
  starting transfers between devices  83.4 us (36%)
  Pallas kernels  60.5 us (26%)
  waiting for transfers between devices  47.2 us (20%)
  blocking collectives  13.1 us (6%)
  other arithmetic  12.9 us (6%)
  local copies, waits for them, and re-layouts  9.13 us (4%)
  matrix products  2.53 us (1%)
    ppermute x1, starting transfers between devices, extended(): lax.ppermute(tail, axis, [(i, (i + 1) % count) for i in range(count)])  69.5 us
    pallas_call x1, Pallas kernels, attend_slots(): pl.pallas_call(functools.partial(attend_kernel, heads=heads, depth=depth)...  60.5 us
    all_to_all x1, waiting for transfers between devices, local(): lax.all_to_all(placed, 'tile', split_axis=0, concat_axis=0, tiled=True)  26.2 us
    all_to_all x1, waiting for transfers between devices, local(): lax.all_to_all(partials, 'obs', split_axis=0, concat_axis=0, tiled=True)  17.1 us
    all_gather x1, blocking collectives, local(): attended = lax.all_gather(attended, 'obs', axis=0, tiled=True)  13.1 us
    all_to_all x1, starting transfers between devices, local(): lax.all_to_all(placed, 'tile', split_axis=0, concat_axis=0, tiled=True)  7.56 us
    all_to_all x1, starting transfers between devices, local(): lax.all_to_all(partials, 'obs', split_axis=0, concat_axis=0, tiled=True)  6.33 us
  transfers between devices with their start and end apart: 4, of which 4 were waited for; matrix products, arithmetic and copies ran while one was open for 2% of the time, Pallas kernels for 0%

commit v1 on v0

--- a/solution.py
+++ b/solution.py
@@ -239,14 +239,11 @@
         factor_o[..., None] * mix_o, axis=0
     )
     attended = (mixture / total[..., None]).reshape(share, model_width).astype(jnp.bfloat16)
-    attended = lax.all_gather(attended, "obs", axis=0, tiled=True)
-
-    column_count = out_weight.shape[1]
-    column_start = lax.axis_index("obs") * column_count
-    latent_columns = lax.dynamic_slice_in_dim(latents, column_start, column_count, 1).astype(
-        jnp.float32
-    )
-    updated = latent_columns + jnp.dot(attended, out_weight, preferred_element_type=jnp.float32)
+    full_out_weight = lax.all_gather(out_weight, "obs", axis=1, tiled=True)
+    updated_rows = latent_mine.astype(jnp.float32) + jnp.dot(
+        attended, full_out_weight, preferred_element_type=jnp.float32
+    )
+    updated = lax.all_to_all(updated_rows, "obs", split_axis=1, concat_axis=0, tiled=True)
     padded = extended(updated, (("tile", 0),), 1)
     return updated + edge_gain[None, :] * (padded[:-2] + padded[2:] - 2.0 * updated)
 

time: 231 us -> 239 us (1.035)
  the two profiles are of different devices: /device:TPU:6 before, /device:TPU:4 now
where the time goes in v1:
time: 239 us; the launch traced here: 236 us
  Pallas kernels  80.9 us (34%)
  waiting for transfers between devices  75.6 us (32%)
  blocking collectives  33.8 us (14%)
  starting transfers between devices  17 us (7%)
  other arithmetic  16.7 us (7%)
  local copies, waits for them, and re-layouts  8.35 us (3%)
  matrix products  3.39 us (1%)
    pallas_call x1, Pallas kernels, attend_slots(): pl.pallas_call(functools.partial(attend_kernel, heads=heads, depth=depth)...  80.9 us
    ppermute x1, waiting for transfers between devices, extended(): lax.ppermute(head, axis, [((i + 1) % count, i) for i in range(count)])  47.3 us
    all_to_all x1, waiting for transfers between devices, local(): lax.all_to_all(placed, 'tile', split_axis=0, concat_axis=0, tiled=True)  26.4 us
    all_gather x1, blocking collectives, local(): full_out_weight = lax.all_gather(out_weight, 'obs', axis=1, tiled=True)  25.1 us
    all_to_all x1, blocking collectives, local(): lax.all_to_all(updated_rows, 'obs', split_axis=1, concat_axis=0, tiled=True)  8.64 us
    all_to_all x1, starting transfers between devices, local(): lax.all_to_all(placed, 'tile', split_axis=0, concat_axis=0, tiled=True)  7.58 us
    all_to_all x1, starting transfers between devices, local(): lax.all_to_all(partials, 'obs', split_axis=0, concat_axis=0, tiled=True)  5.28 us
  transfers between devices with their start and end apart: 4, of which 3 were waited for; matrix products, arithmetic and copies ran while one was open for 2% of the time, Pallas kernels for 0%

profile of v1, /device:TPU:4, one launch (start us, length us, event | category | flops | bytes accessed | tf_op | source)
XLA Modules:
  0.0 235.9 jit_solution(9226218473113054174)
XLA Ops:
  0.0 0.7 broadcast_add_fusion
  0.7 0.7 copy.28
  1.4 0.7 fusion.15
  2.2 0.8 select_reduce_fusion
  3.1 0.7 add_add_fusion
  3.8 0.8 fusion.13
  4.6 1.5 maximum_maximum_fusion
  6.1 0.7 fusion
  6.9 1.7 copy.40
  8.6 7.6 %all-to-all-start = ((bf16[64,136,128]{2,1,0:T(8,128)(2,1)}), bf16[64,136,128]{2,1,0:T(8,128)(2,1)}, u32[]{:S(2)}, u32[]{:S(2)}) async-start(bf16[64,136,128]{2,1,0:T(8,128)(2,1)} %bitcast.16), calls=%async_computation | async-start | bytes 4456448 | tf_op jit(solution)/shard_map/all_to_all | solution.py:196
  16.2 0.9 fusion.18
  17.1 1.0 copy.38
  18.1 1.2 convolution_convert_fusion.1
  19.4 26.4 %all-to-all-done.raw_ref.bias_ref = bf16[64,136,128]{2,1,0:T(8,128)(2,1)} async-done(((bf16[64,136,128]{2,1,0:T(8,128)(2,1)}), bf16[64,136,128]{2,1,0:T(8,128)(2,1)}, u32[]{:S(2)}, u32[]{:S(2)}) %all-to-all-start) | async-done | bytes 2228256 | tf_op jit(solution)/shard_map/all_to_all | solution.py:196
  45.8 0.9 fusion.11
  46.8 0.5 add_bitcast_fusion
  47.3 80.9 %shard_map.127 = (f32[4,128,8]{2,1,0:T(8,128)}, f32[4,128,8]{2,1,0:T(8,128)}, f32[4,128,512]{2,1,0:T(8,128)}) custom-call(s32[64]{0:T(128)} %get-tuple-element.20.kind_ref, s32[64]{0:T(128)} %get-tuple-element.19.tile_ref, bf16[64,136,128]{2,1,0:T(8,128)(2,1)} %all-to-all-done.raw_ref.bias_ref, bf16[64,136,128]{2,1,0:T(8,128)(2,1)} %all-to-all-done.raw_ref.bias_ref, ...), custom_call_target="tpu_custom_call" | custom-call | flops 31138512896 | bytes 8814592 | tf_op jit(solution)/shard_map/pallas_call | solution.py:112
  128.3 2.6 %pad_maximum_fusion = f32[8,64,528]{2,1,0:T(8,128)} fusion(f32[8,64,8]{2,1,0:T(8,128)} %bitcast.40, f32[8,64,8]{2,1,0:T(8,128)} %bitcast.39, f32[8,64,512]{2,1,0:T(8,128)} %bitcast.36), kind=kLoop, calls=%fused_computation.2 | loop fusion | flops 540672 | bytes 2162688 | tf_op jit(solution)/shard_map/concatenate | solution.py:209
  130.9 5.3 %all-to-all-start.1 = ((f32[8,64,528]{2,1,0:T(8,128)}), f32[8,64,528]{2,1,0:T(8,128)S(1)}, u32[]{:S(2)}, u32[]{:S(2)}) async-start(f32[8,64,528]{2,1,0:T(8,128)} %pad_maximum_fusion), calls=%async_computation.1 | async-start | bytes 2621440 | tf_op jit(solution)/shard_map/all_to_all | solution.py:217
  136.2 0.3 convolution_convert_fusion.2
  136.5 0.9 convert_multiply_fusion
  137.3 0.1 mul.80
  137.4 0.1 reduce_sum.36
  137.6 25.1 %all_gather.3 = bf16[512,512]{0,1:T(8,128)(2,1)S(1)} all-gather(bf16[512,64]{0,1:T(8,128)(2,1)} %param.24), channel_id=1, replica_groups=mesh['obs'=8,'tile'=16] {'obs'}, dimensions={1}, use_global_device_ids=true | all-gather | bytes 589824 | tf_op jit(solution)/shard_map/all_gather | solution.py:242
  162.7 0.7 slice_reduce_fusion
  163.4 0.8 fusion.12
  164.2 0.7 fusion.4
  164.9 0.6 mul.89
  165.6 1.5 mul.90
  167.0 0.9 fusion.17
  167.9 0.1 div.11
  168.1 0.1 div.12
  168.2 0.1 mul.86
  168.3 0.1 mul.87
  168.5 1.4 fusion.3
  169.8 1.1 convolution_add_fusion
  171.0 0.1 all_to_all.23
  171.1 0.2 reshape.205
  171.3 8.6 %all_to_all.30 = f32[8,1,4096]{2,1,0:T(1,128)S(1)} all-to-all(f32[8,1,4096]{2,1,0:T(1,128)S(1)} %reshape.205), channel_id=1, replica_groups=mesh['obs'=8,'tile'=16] {'obs'}, dimensions={0} | all-to-all | bytes 262144 | tf_op jit(solution)/shard_map/all_to_all | solution.py:246
  180.0 0.5 broadcast.152
  180.5 1.0 reduce.1
  181.4 0.1 reshape.206
  181.5 0.1 copy.37
  181.7 0.6 collective-permute-start
  182.3 3.5 %collective-permute-start.1 = (f32[1,64]{0,1:T(8,128)S(1)}, f32[1,64]{0,1:T(8,128)S(1)}, u32[]{:S(2)}, u32[]{:S(2)}) collective-permute-start(f32[1,64]{0,1:T(8,128)S(1)} %get-tuple-element.18), channel_id=1, source_target_pairs={{1,0},{2,1},{3,2},{4,3},{5,4},{6,5},{7,6},{8,7},{9,8},{10,9},{11,1... | collective-permute-start | bytes 776 | tf_op jit(solution)/shard_map/ppermute | solution.py:24
  185.9 1.9 collective-permute-done
  187.8 47.3 %collective-permute-done.1 = f32[1,64]{0,1:T(8,128)S(1)} collective-permute-done((f32[1,64]{0,1:T(8,128)S(1)}, f32[1,64]{0,1:T(8,128)S(1)}, u32[]{:S(2)}, u32[]{:S(2)}) %collective-permute-start.1) | collective-permute-done | bytes 288 | tf_op jit(solution)/shard_map/ppermute | solution.py:24
  235.1 0.8 fusion.8
  (24 shorter events, 0.4 us)
Async XLA Ops:
  0.0 18.1 %copy-start = (bf16[512,512]{1,0:T(8,128)(2,1)S(1)}, bf16[512,512]{1,0:T(8,128)(2,1)}, u32[]{:S(2)}) copy-start(bf16[512,512]{1,0:T(8,128)(2,1)} %param.21) | copy-start | bytes 1572868
  8.6 7.6 %copy-start.3 = (bf16[512,1024]{1,0:T(8,128)(2,1)S(1)}, bf16[512,1024]{1,0:T(8,128)(2,1)}, u32[]{:S(2)}) copy-start(bf16[512,1024]{1,0:T(8,128)(2,1)} %param.22) | copy-start | bytes 3145732
  8.6 37.2 %all-to-all-start = ((bf16[64,136,128]{2,1,0:T(8,128)(2,1)}), bf16[64,136,128]{2,1,0:T(8,128)(2,1)}, u32[]{:S(2)}, u32[]{:S(2)}) async-start(bf16[64,136,128]{2,1,0:T(8,128)(2,1)} %bitcast.16), calls=%async_computation | async-start | bytes 4456448 | tf_op jit(solution)/shard_map/all_to_all | solution.py:196
  16.2 1.9 copy-start.4
  130.9 31.8 %all-to-all-start.1 = ((f32[8,64,528]{2,1,0:T(8,128)}), f32[8,64,528]{2,1,0:T(8,128)S(1)}, u32[]{:S(2)}, u32[]{:S(2)}) async-start(f32[8,64,528]{2,1,0:T(8,128)} %pad_maximum_fusion), calls=%async_computation.1 | async-start | bytes 2621440 | tf_op jit(solution)/shard_map/all_to_all | solution.py:217
  136.2 27.3 %copy-start.6 = (f32[8]{0:T(128)S(1)}, f32[8]{0:T(128)}, u32[]{:S(2)}) copy-start(f32[8]{0:T(128)} %param.23) | copy-start | bytes 100
  137.6 25.8 %copy-start.5 = (f32[64,8]{1,0:T(8,128)}, f32[64,8]{1,0:T(8,128)S(1)}, u32[]{:S(2)}) copy-start(f32[64,8]{1,0:T(8,128)S(1)} %reduce_sum.36) | copy-start | bytes 6148
  162.7 2.2 copy-start.1
  167.0 1.4 copy-start.2
  171.0 64.1 %copy-start.7 = (f32[64]{0:T(128)S(1)}, f32[64]{0:T(128)}, u32[]{:S(2)}) copy-start(f32[64]{0:T(128)} %param.25) | copy-start | bytes 772
  181.7 6.0 %collective-permute-start = (f32[1,64]{0,1:T(8,128)S(1)}, f32[1,64]{0,1:T(8,128)S(1)}, u32[]{:S(2)}, u32[]{:S(2)}) collective-permute-start(f32[1,64]{0,1:T(8,128)S(1)} %get-tuple-element.17), channel_id=1, source_target_pairs={{0,1},{1,2},{2,3},{3,4},{4,5},{5,6},{6,7},{7,8},{8,9},{9,10},{10,1... | collective-permute-start | bytes 776 | tf_op jit(solution)/shard_map/ppermute | solution.py:22
  182.3 52.7 %collective-permute-start.1 = (f32[1,64]{0,1:T(8,128)S(1)}, f32[1,64]{0,1:T(8,128)S(1)}, u32[]{:S(2)}, u32[]{:S(2)}) collective-permute-start(f32[1,64]{0,1:T(8,128)S(1)} %get-tuple-element.18), channel_id=1, source_target_pairs={{1,0},{2,1},{3,2},{4,3},{5,4},{6,5},{7,6},{8,7},{9,8},{10,9},{11,1... | collective-permute-start | bytes 776 | tf_op jit(solution)/shard_map/ppermute | solution.py:24

commit v2 on v0

--- a/solution.py
+++ b/solution.py
@@ -206,19 +206,25 @@
 
     row_total = latents.shape[0]
     share = row_total // obs_count
+    stats = jnp.concatenate(
+        [part_peak.reshape(row_total, head_count), part_sum.reshape(row_total, head_count)], axis=1
+    )
+    stat_rows = -(-share * 2 * head_count // model_width)
+    stats = stats.reshape(obs_count, share * 2 * head_count)
+    stats = jnp.pad(stats, ((0, 0), (0, stat_rows * model_width - share * 2 * head_count)))
     partials = jnp.concatenate(
         [
-            part_mix.reshape(row_total, model_width),
-            part_peak.reshape(row_total, head_count),
-            part_sum.reshape(row_total, head_count),
+            part_mix.reshape(obs_count, share, model_width),
+            stats.reshape(obs_count, stat_rows, model_width),
         ],
         axis=1,
     )
     mine = lax.all_to_all(partials, "obs", split_axis=0, concat_axis=0, tiled=True)
-    mine = mine.reshape(obs_count, share, model_width + 2 * head_count)
-    mix_o = mine[..., :model_width].reshape(obs_count, share, head_count, head_depth)
-    peak_o = mine[..., model_width:model_width + head_count]
-    sum_o = mine[..., model_width + head_count:]
+    mix_o = mine[:, :share].reshape(obs_count, share, head_count, head_depth)
+    stats_o = mine[:, share:].reshape(obs_count, stat_rows * model_width)[:, :share * 2 * head_count]
+    stats_o = stats_o.reshape(obs_count, share, 2 * head_count)
+    peak_o = stats_o[..., :head_count]
+    sum_o = stats_o[..., head_count:]
 
     row_start = lax.axis_index("obs") * share
     latent_mine = lax.dynamic_slice_in_dim(latents, row_start, share, 0)

time: 231 us -> 231 us (level)
  the two profiles are of different devices: /device:TPU:6 before, /device:TPU:24 now
where the time goes in v2:
time: 231 us; the launch traced here: 229 us
  Pallas kernels  131 us (57%)
  waiting for transfers between devices  45.7 us (20%)
  starting transfers between devices  14.6 us (6%)
  blocking collectives  13.1 us (6%)
  other arithmetic  12.7 us (5%)
  local copies, waits for them, and re-layouts  9.18 us (4%)
  matrix products  2.54 us (1%)
    pallas_call x1, Pallas kernels, attend_slots(): pl.pallas_call(functools.partial(attend_kernel, heads=heads, depth=depth)...  131 us
    all_to_all x1, waiting for transfers between devices, local(): lax.all_to_all(placed, 'tile', split_axis=0, concat_axis=0, tiled=True)  25.9 us
    all_to_all x1, waiting for transfers between devices, local(): lax.all_to_all(partials, 'obs', split_axis=0, concat_axis=0, tiled=True)  15.7 us
    all_gather x1, blocking collectives, local(): attended = lax.all_gather(attended, 'obs', axis=0, tiled=True)  13.1 us
    all_to_all x1, starting transfers between devices, local(): lax.all_to_all(placed, 'tile', split_axis=0, concat_axis=0, tiled=True)  7.3 us
    all_to_all x1, starting transfers between devices, local(): lax.all_to_all(partials, 'obs', split_axis=0, concat_axis=0, tiled=True)  5.27 us
  transfers between devices with their start and end apart: 4, of which 4 were waited for; matrix products, arithmetic and copies ran while one was open for 2% of the time, Pallas kernels for 0%

profile of v2, /device:TPU:24, one launch (start us, length us, event | category | flops | bytes accessed | tf_op | source)
XLA Modules:
  0.0 228.6 jit_solution(17862652296671173973)
XLA Ops:
  0.0 0.7 broadcast_add_fusion
  0.7 0.7 copy.34
  1.4 0.7 fusion.14
  2.2 0.8 select_reduce_fusion
  3.1 0.7 add_add_fusion
  3.7 0.1 pad.11.clone
  3.8 0.8 fusion.12
  4.6 1.5 maximum_maximum_fusion
  6.1 0.7 fusion
  6.9 1.7 copy.40
  8.6 7.3 %all-to-all-start = ((bf16[64,136,128]{2,1,0:T(8,128)(2,1)}), bf16[64,136,128]{2,1,0:T(8,128)(2,1)}, u32[]{:S(2)}, u32[]{:S(2)}) async-start(bf16[64,136,128]{2,1,0:T(8,128)(2,1)} %bitcast.13), calls=%async_computation | async-start | bytes 4456448 | tf_op jit(solution)/shard_map/all_to_all | solution.py:196
  15.9 0.9 fusion.17
  16.8 1.0 copy.38
  17.8 1.2 convolution_convert_fusion.1
  19.0 25.9 %all-to-all-done.raw_ref.bias_ref = bf16[64,136,128]{2,1,0:T(8,128)(2,1)} async-done(((bf16[64,136,128]{2,1,0:T(8,128)(2,1)}), bf16[64,136,128]{2,1,0:T(8,128)(2,1)}, u32[]{:S(2)}, u32[]{:S(2)}) %all-to-all-start) | async-done | bytes 2228256 | tf_op jit(solution)/shard_map/all_to_all | solution.py:196
  45.0 0.9 fusion.10
  45.9 0.1 copy.35
  46.0 0.5 add_bitcast_fusion
  46.5 130.6 %shard_map.127 = (f32[4,128,8]{2,1,0:T(8,128)}, f32[4,128,8]{2,1,0:T(8,128)}, f32[4,128,512]{2,1,0:T(8,128)}) custom-call(s32[64]{0:T(128)} %get-tuple-element.20.kind_ref, s32[64]{0:T(128)} %get-tuple-element.19.tile_ref, bf16[64,136,128]{2,1,0:T(8,128)(2,1)} %all-to-all-done.raw_ref.bias_ref, bf16[64,136,128]{2,1,0:T(8,128)(2,1)} %all-to-all-done.raw_ref.bias_ref, ...), custom_call_target="tpu_custom_call" | custom-call | flops 31138512896 | bytes 8814592 | tf_op jit(solution)/shard_map/pallas_call | solution.py:112
  177.1 1.3 pad_maximum_fusion.1
  178.4 0.2 reshape.206
  178.5 1.1 pad_maximum_fusion
  179.7 5.3 %all-to-all-start.1 = ((f32[8,66,512]{2,1,0:T(8,128)}), f32[8,66,512]{2,1,0:T(8,128)S(1)}, u32[]{:S(2)}, u32[]{:S(2)}) async-start(f32[8,66,512]{2,1,0:T(8,128)} %pad_maximum_fusion), calls=%async_computation.1 | async-start | bytes 2359296 | tf_op jit(solution)/shard_map/all_to_all | solution.py:222
  184.9 0.3 convolution_convert_fusion.2
  185.3 0.9 convert_multiply_fusion
  186.1 0.1 mul.81
  186.2 0.1 constant_dynamic-slice_fusion
  186.3 0.1 copy.37
  186.4 0.1 reduce_sum.36
  186.6 15.7 %all-to-all-done.1 = f32[8,66,512]{2,1,0:T(8,128)S(1)} async-done(((f32[8,66,512]{2,1,0:T(8,128)}), f32[8,66,512]{2,1,0:T(8,128)S(1)}, u32[]{:S(2)}, u32[]{:S(2)}) %all-to-all-start.1) | async-done | bytes 1081376 | tf_op jit(solution)/shard_map/all_to_all | solution.py:222
  202.3 0.1 reshape_reshape.3
  202.5 0.1 fusion.4
  202.6 0.7 copy-done.1
  203.3 0.6 mul.90
  203.9 1.5 mul.91
  205.4 0.1 div.11
  205.5 0.1 div.12
  205.7 0.1 mul.87
  205.8 0.1 mul.88
  205.9 0.8 copy-done.2
  206.7 1.5 fusion.3
  208.2 13.1 %all_gather.3 = bf16[512,512]{1,0:T(8,128)(2,1)S(1)} all-gather(bf16[64,512]{1,0:T(8,128)(2,1)S(1)} %divide_convert_fusion), channel_id=1, replica_groups=mesh['obs'=8,'tile'=16] {'obs'}, dimensions={0}, use_global_device_ids=true | all-gather | bytes 589824 | tf_op jit(solution)/shard_map/all_gather | solution.py:248
  221.3 0.3 convolution_add_fusion
  221.6 0.1 fusion.18
  221.7 2.0 collective-permute-start.1
  223.7 1.9 collective-permute-done
  225.6 2.2 collective-permute-done.1
  227.8 0.8 fusion.8
  (25 shorter events, 0.2 us)
Async XLA Ops:
  0.0 17.8 %copy-start = (bf16[512,512]{1,0:T(8,128)(2,1)S(1)}, bf16[512,512]{1,0:T(8,128)(2,1)}, u32[]{:S(2)}) copy-start(bf16[512,512]{1,0:T(8,128)(2,1)} %param.18) | copy-start | bytes 1572868
  8.6 7.3 %copy-start.3 = (bf16[512,1024]{1,0:T(8,128)(2,1)S(1)}, bf16[512,1024]{1,0:T(8,128)(2,1)}, u32[]{:S(2)}) copy-start(bf16[512,1024]{1,0:T(8,128)(2,1)} %param.22) | copy-start | bytes 3145732
  8.6 36.4 %all-to-all-start = ((bf16[64,136,128]{2,1,0:T(8,128)(2,1)}), bf16[64,136,128]{2,1,0:T(8,128)(2,1)}, u32[]{:S(2)}, u32[]{:S(2)}) async-start(bf16[64,136,128]{2,1,0:T(8,128)(2,1)} %bitcast.13), calls=%async_computation | async-start | bytes 4456448 | tf_op jit(solution)/shard_map/all_to_all | solution.py:196
  15.9 1.9 copy-start.5
  177.1 1.4 copy-start.4
  179.7 22.6 %all-to-all-start.1 = ((f32[8,66,512]{2,1,0:T(8,128)}), f32[8,66,512]{2,1,0:T(8,128)S(1)}, u32[]{:S(2)}, u32[]{:S(2)}) async-start(f32[8,66,512]{2,1,0:T(8,128)} %pad_maximum_fusion), calls=%async_computation.1 | async-start | bytes 2359296 | tf_op jit(solution)/shard_map/all_to_all | solution.py:222
  185.2 17.2 %copy-start.7 = (f32[8]{0:T(128)S(1)}, f32[8]{0:T(128)}, u32[]{:S(2)}) copy-start(f32[8]{0:T(128)} %param.23) | copy-start | bytes 100
  202.3 1.0 copy-start.1
  205.4 1.3 copy-start.2
  206.7 14.6 %copy-start.6 = (bf16[512,64]{0,1:T(8,128)(2,1)S(1)}, bf16[512,64]{0,1:T(8,128)(2,1)}, u32[]{:S(2)}) copy-start(bf16[512,64]{0,1:T(8,128)(2,1)} %param.24) | copy-start | bytes 196612
  208.1 19.7 %copy-start.8 = (f32[64]{0:T(128)S(1)}, f32[64]{0:T(128)}, u32[]{:S(2)}) copy-start(f32[64]{0:T(128)} %param.25) | copy-start | bytes 772
  221.7 3.9 %collective-permute-start = (f32[1,64]{0,1:T(8,128)S(1)}, f32[1,64]{0,1:T(8,128)S(1)}, u32[]{:S(2)}, u32[]{:S(2)}) collective-permute-start(f32[1,64]{0,1:T(8,128)S(1)} %get-tuple-element.17), channel_id=1, source_target_pairs={{0,1},{1,2},{2,3},{3,4},{4,5},{5,6},{6,7},{7,8},{8,9},{9,10},{10,1... | collective-permute-start | bytes 776 | tf_op jit(solution)/shard_map/ppermute | solution.py:22
  221.7 6.1 %collective-permute-start.1 = (f32[1,64]{0,1:T(8,128)S(1)}, f32[1,64]{0,1:T(8,128)S(1)}, u32[]{:S(2)}, u32[]{:S(2)}) collective-permute-start(f32[1,64]{0,1:T(8,128)S(1)} %get-tuple-element.18), channel_id=1, source_target_pairs={{1,0},{2,1},{3,2},{4,3},{5,4},{6,5},{7,6},{8,7},{9,8},{10,9},{11,1... | collective-permute-start | bytes 776 | tf_op jit(solution)/shard_map/ppermute | solution.py:24
